TPU v7x, 512 devices: a whole 4x4x16 slice. The times are simulated.
512 devices in a mesh: ctx: 64 (over z, y_hi, core), chan: 8 (over x, y_lo).
Axes of the slice: x: 4, y: 4 (y_hi: 2, y_lo: 2; y = y_hi * 2 + y_lo), z: 16, core: 2. Of those that a mesh axis runs over, the one named last changes fastest.
Arguments:
- query_pol: bfloat16 [8192, 8192], P('chan', 'ctx'), may hold values from -6 to 6
- keys_pol: bfloat16 [8192, 8192], P('chan', 'ctx'), may hold values from -6 to 6
- value_pol: bfloat16 [8192, 8192], P('chan', 'ctx'), may hold values from -6 to 6
- filter_pol: float32 [4, 8192], P(None, 'ctx'), may hold values from -1.2 to 1.2
- skip_pol: float32 [8192], P('chan'), may hold values from -4 to 4
- query_ref: bfloat16 [8192, 8192], P('chan', 'ctx'), may hold values from -6 to 6
- keys_ref: bfloat16 [8192, 8192], P('chan', 'ctx'), may hold values from -6 to 6
- value_ref: bfloat16 [8192, 8192], P('chan', 'ctx'), may hold values from -6 to 6
- filter_ref: float32 [4, 8192], P(None, 'ctx'), may hold values from -1.2 to 1.2
- skip_ref: float32 [8192], P('chan'), may hold values from -4 to 4
- grad_out: bfloat16 [8192, 8192], P('chan', 'ctx'), may hold values from -0.75 to 0.75
Outputs:
- out_pol: bfloat16 [8192, 8192], P('chan', 'ctx')
- out_ref: bfloat16 [8192, 8192], P('chan', 'ctx')
- grad_query: bfloat16 [8192, 8192], P('chan', 'ctx')
- grad_keys: bfloat16 [8192, 8192], P('chan', 'ctx')
- grad_value: bfloat16 [8192, 8192], P('chan', 'ctx')
- grad_filter: float32 [4, 8192], P(None, 'ctx')
All inputs are finite; a program needn't handle non-finite values.
Results may differ from a plain program's by a relative error of at most 0.003.
Values sent between devices are 32-bit elements; how exact they have to be, the bound alone decides.
No kernel may reach another device: no remote copies, remote signals or barrier semaphores. Data moves between devices by JAX's collectives and lax.ppermute only.
A program may use at most 64 MiB of HBM per device.

v0:
```python
import math

import jax
import jax.numpy as jnp
from jax import lax
from jax.sharding import PartitionSpec as P

HIGHEST = lax.Precision.HIGHEST


def phase_table(row_count, col_count, period, col_start):
    left_index = jnp.arange(row_count, dtype=jnp.int32)[:, None]
    right_index = jnp.arange(col_count, dtype=jnp.int32)[None, :] + col_start
    turns = (left_index * right_index % period).astype(jnp.float32) * (2.0 * math.pi / period)
    return (jnp.cos(turns), jnp.sin(turns))


def forward_spectrum(fields):
    row_count, seq_width = fields.shape
    shard_count = lax.axis_size("ctx")
    span_width = seq_width // shard_count
    block_count = 2 * shard_count
    full_length = block_count * seq_width
    columns = jnp.transpose(fields).reshape(1, seq_width, row_count)
    by_position = lax.all_to_all(columns, "ctx", split_axis=1, concat_axis=0, tiled=True)
    cos_block, sin_block = phase_table(shard_count, block_count, block_count, 0)
    real_part = jnp.einsum("amr,ak->kmr", by_position, cos_block, precision=HIGHEST)
    imag_part = -jnp.einsum("amr,ak->kmr", by_position, sin_block, precision=HIGHEST)
    first_pos = lax.axis_index("ctx") * span_width
    twist_cos, twist_sin = phase_table(block_count, span_width, full_length, first_pos)
    twist_cos = twist_cos[:, :, None]
    twist_sin = twist_sin[:, :, None]
    turned_real = real_part * twist_cos + imag_part * twist_sin
    turned_imag = imag_part * twist_cos - real_part * twist_sin
    moved_real, moved_imag = (
        lax.all_to_all(turned_real, "ctx", split_axis=0, concat_axis=1, tiled=True),
        lax.all_to_all(turned_imag, "ctx", split_axis=0, concat_axis=1, tiled=True),
    )
    cos_local, sin_local = phase_table(seq_width, seq_width, seq_width, 0)
    spec_real = jnp.einsum("pnr,nf->pfr", moved_real, cos_local, precision=HIGHEST) + jnp.einsum(
        "pnr,nf->pfr", moved_imag, sin_local, precision=HIGHEST
    )
    spec_imag = jnp.einsum("pnr,nf->pfr", moved_imag, cos_local, precision=HIGHEST) - jnp.einsum(
        "pnr,nf->pfr", moved_real, sin_local, precision=HIGHEST
    )
    return (jnp.transpose(spec_real, (2, 0, 1)), jnp.transpose(spec_imag, (2, 0, 1)))


def inverse_field(spec_real, spec_imag):
    row_count, pair_count, seq_width = spec_real.shape
    shard_count = lax.axis_size("ctx")
    span_width = seq_width // shard_count
    block_count = 2 * shard_count
    full_length = block_count * seq_width
    cos_local, sin_local = phase_table(seq_width, seq_width, seq_width, 0)
    lead_real = jnp.transpose(spec_real, (1, 2, 0))
    lead_imag = jnp.transpose(spec_imag, (1, 2, 0))
    back_real = jnp.einsum("pfr,fn->pnr", lead_real, cos_local, precision=HIGHEST) - jnp.einsum(
        "pfr,fn->pnr", lead_imag, sin_local, precision=HIGHEST
    )
    back_imag = jnp.einsum("pfr,fn->pnr", lead_real, sin_local, precision=HIGHEST) + jnp.einsum(
        "pfr,fn->pnr", lead_imag, cos_local, precision=HIGHEST
    )
    moved_real, moved_imag = (
        lax.all_to_all(back_real, "ctx", split_axis=1, concat_axis=0, tiled=True),
        lax.all_to_all(back_imag, "ctx", split_axis=1, concat_axis=0, tiled=True),
    )
    first_pos = lax.axis_index("ctx") * span_width
    twist_cos, twist_sin = phase_table(block_count, span_width, full_length, first_pos)
    twist_cos = twist_cos[:, :, None]
    twist_sin = twist_sin[:, :, None]
    turned_real = moved_real * twist_cos - moved_imag * twist_sin
    turned_imag = moved_real * twist_sin + moved_imag * twist_cos
    cos_block, sin_block = phase_table(block_count, shard_count, block_count, 0)
    local_values = jnp.einsum("kmr,ka->amr", turned_real, cos_block, precision=HIGHEST)
    local_values = (
        local_values - jnp.einsum("kmr,ka->amr", turned_imag, sin_block, precision=HIGHEST)
    ) / full_length
    returned = lax.all_to_all(local_values, "ctx", split_axis=0, concat_axis=1, tiled=True)
    return jnp.transpose(returned.reshape(seq_width, row_count))


def combine_filter(field_real, field_imag, filt_real, filt_imag, conjugate):
    row_count, pair_count, seq_width = field_real.shape
    group_count = filt_real.shape[0]
    grouped_shape = (row_count // group_count, group_count, pair_count, seq_width)
    grouped_real = field_real.reshape(grouped_shape)
    grouped_imag = field_imag.reshape(grouped_shape)
    if conjugate:
        result_real = grouped_real * filt_real + grouped_imag * filt_imag
        result_imag = grouped_imag * filt_real - grouped_real * filt_imag
    else:
        result_real = grouped_real * filt_real - grouped_imag * filt_imag
        result_imag = grouped_real * filt_imag + grouped_imag * filt_real
    full_shape = (row_count, pair_count, seq_width)
    return (result_real.reshape(full_shape), result_imag.reshape(full_shape))


def local(
    query_pol,
    keys_pol,
    value_pol,
    filter_pol,
    skip_pol,
    query_ref,
    keys_ref,
    value_ref,
    filter_ref,
    skip_ref,
    grad_out,
):
    chan_rows, seq_width = query_pol.shape
    group_count = filter_pol.shape[0]
    two_rows = 2 * chan_rows
    gated_pol = keys_pol.astype(jnp.float32) * value_pol.astype(jnp.float32)
    gated_ref = keys_ref.astype(jnp.float32) * value_ref.astype(jnp.float32)
    stacked = jnp.concatenate([gated_pol, gated_ref, filter_pol, filter_ref], axis=0)
    spec_real, spec_imag = forward_spectrum(stacked)
    saved_real = spec_real[:chan_rows]
    saved_imag = spec_imag[:chan_rows]
    hpol_real = spec_real[two_rows : two_rows + group_count]
    hpol_imag = spec_imag[two_rows : two_rows + group_count]
    href_real = spec_real[two_rows + group_count :]
    href_imag = spec_imag[two_rows + group_count :]
    conv_pol = combine_filter(saved_real, saved_imag, hpol_real, hpol_imag, False)
    conv_ref = combine_filter(
        spec_real[chan_rows:two_rows], spec_imag[chan_rows:two_rows], href_real, href_imag, False
    )
    fields = inverse_field(
        jnp.concatenate([conv_pol[0], conv_ref[0]], axis=0),
        jnp.concatenate([conv_pol[1], conv_ref[1]], axis=0),
    )
    field_pol = fields[:chan_rows]
    field_ref = fields[chan_rows:]
    mix_pol = field_pol + skip_pol[:, None] * gated_pol
    mix_ref = field_ref + skip_ref[:, None] * gated_ref
    out_pol = (query_pol.astype(jnp.float32) * mix_pol).astype(jnp.bfloat16)
    out_ref = (query_ref.astype(jnp.float32) * mix_ref).astype(jnp.bfloat16)
    out_grad = grad_out.astype(jnp.float32)
    grad_sum = out_grad * query_pol.astype(jnp.float32)
    grad_real, grad_imag = forward_spectrum(grad_sum)
    back_real, back_imag = combine_filter(grad_real, grad_imag, hpol_real, hpol_imag, True)
    grouped_shape = (chan_rows // group_count, group_count, 2, seq_width)
    grad_group_real = grad_real.reshape(grouped_shape)
    grad_group_imag = grad_imag.reshape(grouped_shape)
    saved_group_real = saved_real.reshape(grouped_shape)
    saved_group_imag = saved_imag.reshape(grouped_shape)
    cross_real = jnp.sum(
        grad_group_real * saved_group_real + grad_group_imag * saved_group_imag, axis=0
    )
    cross_imag = jnp.sum(
        grad_group_imag * saved_group_real - grad_group_real * saved_group_imag, axis=0
    )
    total_real, total_imag = lax.psum((cross_real, cross_imag), "chan")
    back_fields = inverse_field(
        jnp.concatenate([back_real, total_real], axis=0),
        jnp.concatenate([back_imag, total_imag], axis=0),
    )
    grad_filter = back_fields[chan_rows:]
    grad_mix = back_fields[:chan_rows] + skip_pol[:, None] * grad_sum
    grad_query = (out_grad * mix_pol).astype(jnp.bfloat16)
    grad_keys = (grad_mix * value_pol.astype(jnp.float32)).astype(jnp.bfloat16)
    grad_value = (grad_mix * keys_pol.astype(jnp.float32)).astype(jnp.bfloat16)
    return (out_pol, out_ref, grad_query, grad_keys, grad_value, grad_filter)


def solution(mesh):
    in_specs = (
        P("chan", "ctx"),
        P("chan", "ctx"),
        P("chan", "ctx"),
        P(None, "ctx"),
        P("chan"),
        P("chan", "ctx"),
        P("chan", "ctx"),
        P("chan", "ctx"),
        P(None, "ctx"),
        P("chan"),
        P("chan", "ctx"),
    )
    out_specs = (
        P("chan", "ctx"),
        P("chan", "ctx"),
        P("chan", "ctx"),
        P("chan", "ctx"),
        P("chan", "ctx"),
        P(None, "ctx"),
    )
    return jax.shard_map(local, mesh=mesh, in_specs=in_specs, out_specs=out_specs, check_vma=False)
```

profile of v0, /device:TPU:6, one launch (start us, length us, event | category | flops | bytes accessed | tf_op | source)
XLA Modules:
  0.0 977.5 jit_solution(4095159069237134881)
XLA Ops:
  4.4 18.7 %all-to-all-start.6 = ((f32[1,128,1024]{2,0,1:T(1,128)}), f32[1,128,1024]{2,0,1:T(1,128)S(1)}, u32[]{:S(2)}, u32[]{:S(2)}) async-start(f32[1,128,1024]{2,0,1:T(1,128)} %copy.131), calls=%async_computation.6 | async-start | bytes 1048576 | tf_op jit(solution)/shard_map/all_to_all | solution.py:25
  27.0 29.8 %all-to-all-done.6 = f32[1,128,1024]{2,0,1:T(1,128)S(1)} async-done(((f32[1,128,1024]{2,0,1:T(1,128)}), f32[1,128,1024]{2,0,1:T(1,128)S(1)}, u32[]{:S(2)}, u32[]{:S(2)}) %all-to-all-start.6) | async-done | bytes 524320 | tf_op jit(solution)/shard_map/all_to_all | solution.py:25
  68.2 52.2 %all-to-all-done = f32[1,128,2056]{2,0,1:T(1,128)S(1)} async-done(((f32[1,128,2056]{2,0,1:T(1,128)}), f32[1,128,2056]{2,0,1:T(1,128)S(1)}, u32[]{:S(2)}, u32[]{:S(2)}) %all-to-all-start) | async-done | bytes 1052704 | tf_op jit(solution)/shard_map/all_to_all | solution.py:25
  120.4 6.2 all-to-all-start.8
  128.4 53.2 %all-to-all-done.8 = f32[128,2,1024]{2,1,0:T(2,128)} async-done(((f32[128,2,1024]{2,1,0:T(2,128)}), f32[128,2,1024]{2,1,0:T(2,128)}, u32[]{:S(2)}, u32[]{:S(2)}) %all-to-all-start.8) | async-done | bytes 1048608 | tf_op jit(solution)/shard_map/all_to_all | solution.py:37
  181.6 6.9 all-to-all-start.7
  203.8 39.8 %all-to-all-done.7 = f32[128,2,1024]{2,1,0:T(2,128)} async-done(((f32[128,2,1024]{2,1,0:T(2,128)}), f32[128,2,1024]{2,1,0:T(2,128)}, u32[]{:S(2)}, u32[]{:S(2)}) %all-to-all-start.7) | async-done | bytes 1048608 | tf_op jit(solution)/shard_map/all_to_all | solution.py:36
  243.6 6.4 all-to-all-start.1
  254.6 102.1 %all-to-all-done.1 = f32[128,2,2056]{2,1,0:T(2,128)S(1)} async-done(((f32[128,2,2056]{2,1,0:T(2,128)}), f32[128,2,2056]{2,1,0:T(2,128)S(1)}, u32[]{:S(2)}, u32[]{:S(2)}) %all-to-all-start.1) | async-done | bytes 2105376 | tf_op jit(solution)/shard_map/all_to_all | solution.py:36
  358.0 5.5 all-to-all-start.2
  385.3 84.9 %all-to-all-done.2 = f32[128,2,2056]{2,1,0:T(2,128)} async-done(((f32[128,2,2056]{2,1,0:T(2,128)}), f32[128,2,2056]{2,1,0:T(2,128)}, u32[]{:S(2)}, u32[]{:S(2)}) %all-to-all-start.2) | async-done | bytes 2105376 | tf_op jit(solution)/shard_map/all_to_all | solution.py:37
  497.6 15.8 %all-reduce = (f32[4,2,128]{2,0,1:T(4,128)S(1)}, f32[4,2,128]{2,0,1:T(4,128)S(1)}) all-reduce(f32[4,2,128]{2,0,1:T(4,128)S(1)} %reduce_sum.18, f32[4,2,128]{2,0,1:T(4,128)S(1)} %reduce_sum.19), channel_id=1, replica_groups=mesh['ctx'=64,'chan'=8] {'chan'}, use_global_device_ids=true, to_apply=%region_1.2 | all-reduce | flops 2048 | bytes 16384 | tf_op jit(solution)/shard_map/psum | solution.py:154
  520.2 6.1 all-to-all-start.9
  531.0 57.0 %all-to-all-done.9 = f32[2,128,1028]{2,0,1:T(2,128)} async-done(((f32[2,128,1028]{2,0,1:T(2,128)}), f32[2,128,1028]{2,0,1:T(2,128)}, u32[]{:S(2)}, u32[]{:S(2)}) %all-to-all-start.9) | async-done | bytes 1052704 | tf_op jit(solution)/shard_map/all_to_all | solution.py:65
  587.9 5.5 all-to-all-start.10
  602.3 52.8 %all-to-all-done.10 = f32[2,128,1028]{2,0,1:T(2,128)} async-done(((f32[2,128,1028]{2,0,1:T(2,128)}), f32[2,128,1028]{2,0,1:T(2,128)}, u32[]{:S(2)}, u32[]{:S(2)}) %all-to-all-start.10) | async-done | bytes 1052704 | tf_op jit(solution)/shard_map/all_to_all | solution.py:66
  655.1 6.0 all-to-all-start.3
  669.6 92.3 %all-to-all-done.3 = f32[2,128,2048]{2,0,1:T(2,128)} async-done(((f32[2,128,2048]{2,0,1:T(2,128)}), f32[2,128,2048]{2,0,1:T(2,128)}, u32[]{:S(2)}, u32[]{:S(2)}) %all-to-all-start.3) | async-done | bytes 2097184 | tf_op jit(solution)/shard_map/all_to_all | solution.py:65
  761.9 5.3 all-to-all-start.4
  775.6 92.6 %all-to-all-done.4 = f32[2,128,2048]{2,0,1:T(2,128)S(1)} async-done(((f32[2,128,2048]{2,0,1:T(2,128)}), f32[2,128,2048]{2,0,1:T(2,128)S(1)}, u32[]{:S(2)}, u32[]{:S(2)}) %all-to-all-start.4) | async-done | bytes 2097184 | tf_op jit(solution)/shard_map/all_to_all | solution.py:66
  868.3 5.3 all-to-all-start.11
  893.2 16.8 %all-to-all-done.11 = f32[64,2,1028]{2,1,0:T(2,128)S(1)} async-done(((f32[64,2,1028]{2,1,0:T(2,128)}), f32[64,2,1028]{2,1,0:T(2,128)S(1)}, u32[]{:S(2)}, u32[]{:S(2)}) %all-to-all-start.11) | async-done | bytes 526368 | tf_op jit(solution)/shard_map/all_to_all | solution.py:79
  910.0 5.3 all-to-all-start.5
  917.3 53.2 %all-to-all-done.5 = f32[64,2,2048]{2,1,0:T(2,128)S(1)} async-done(((f32[64,2,2048]{2,1,0:T(2,128)}), f32[64,2,2048]{2,1,0:T(2,128)S(1)}, u32[]{:S(2)}, u32[]{:S(2)}) %all-to-all-start.5) | async-done | bytes 1048608 | tf_op jit(solution)/shard_map/all_to_all | solution.py:79
  (142 shorter events, 156.0 us)
Async XLA Ops:
  0.6 22.5 %copy-start.17 = (bf16[1024,128]{1,0:T(8,128)(2,1)S(1)}, bf16[1024,128]{1,0:T(8,128)(2,1)}, u32[]{:S(2)}) copy-start(bf16[1024,128]{1,0:T(8,128)(2,1)} %param.13) | copy-start | bytes 786436
  1.8 21.5 %copy-start.18 = (bf16[1024,128]{1,0:T(8,128)(2,1)S(1)}, bf16[1024,128]{1,0:T(8,128)(2,1)}, u32[]{:S(2)}) copy-start(bf16[1024,128]{1,0:T(8,128)(2,1)} %param.17) | copy-start | bytes 786436
  2.9 20.6 %copy-start.11 = (bf16[1024,128]{0,1:T(8,128)(2,1)}, bf16[1024,128]{0,1:T(8,128)(2,1)S(1)}, u32[]{:S(2)}) copy-start(bf16[1024,128]{0,1:T(8,128)(2,1)S(1)} %copy.98) | copy-start | bytes 786436
  2.9 20.6 %copy-start.19 = (bf16[1024,128]{1,0:T(8,128)(2,1)S(1)}, bf16[1024,128]{1,0:T(8,128)(2,1)}, u32[]{:S(2)}) copy-start(bf16[1024,128]{1,0:T(8,128)(2,1)} %param.18) | copy-start | bytes 786436
  3.0 20.7 %copy-start.20 = (bf16[1024,128]{1,0:T(8,128)(2,1)S(1)}, bf16[1024,128]{1,0:T(8,128)(2,1)}, u32[]{:S(2)}) copy-start(bf16[1024,128]{1,0:T(8,128)(2,1)} %param.12) | copy-start | bytes 786436
  3.0 20.8 %copy-start.24 = (f32[4,128]{1,0:T(4,128)S(1)}, f32[4,128]{1,0:T(4,128)}, u32[]{:S(2)}) copy-start(f32[4,128]{1,0:T(4,128)} %param.14) | copy-start | bytes 6148
  3.0 20.9 %copy-start.25 = (f32[4,128]{1,0:T(4,128)S(1)}, f32[4,128]{1,0:T(4,128)}, u32[]{:S(2)}) copy-start(f32[4,128]{1,0:T(4,128)} %param.19) | copy-start | bytes 6148
  4.4 52.4 %all-to-all-start.6 = ((f32[1,128,1024]{2,0,1:T(1,128)}), f32[1,128,1024]{2,0,1:T(1,128)S(1)}, u32[]{:S(2)}, u32[]{:S(2)}) async-start(f32[1,128,1024]{2,0,1:T(1,128)} %copy.131), calls=%async_computation.6 | async-start | bytes 1048576 | tf_op jit(solution)/shard_map/all_to_all | solution.py:25
  56.8 63.6 %all-to-all-start = ((f32[1,128,2056]{2,0,1:T(1,128)}), f32[1,128,2056]{2,0,1:T(1,128)S(1)}, u32[]{:S(2)}, u32[]{:S(2)}) async-start(f32[1,128,2056]{2,0,1:T(1,128)} %copy.105), calls=%async_computation | async-start | bytes 2228224 | tf_op jit(solution)/shard_map/all_to_all | solution.py:25
  120.4 61.2 %all-to-all-start.8 = ((f32[128,2,1024]{2,1,0:T(2,128)}), f32[128,2,1024]{2,1,0:T(2,128)}, u32[]{:S(2)}, u32[]{:S(2)}) async-start(f32[128,2,1024]{2,1,0:T(2,128)} %copy.137), calls=%async_computation.8 | async-start | bytes 2097152 | tf_op jit(solution)/shard_map/all_to_all | solution.py:37
  181.6 62.0 %all-to-all-start.7 = ((f32[128,2,1024]{2,1,0:T(2,128)}), f32[128,2,1024]{2,1,0:T(2,128)}, u32[]{:S(2)}, u32[]{:S(2)}) async-start(f32[128,2,1024]{2,1,0:T(2,128)} %copy.134), calls=%async_computation.7 | async-start | bytes 2097152 | tf_op jit(solution)/shard_map/all_to_all | solution.py:36
  243.6 113.0 %all-to-all-start.1 = ((f32[128,2,2056]{2,1,0:T(2,128)}), f32[128,2,2056]{2,1,0:T(2,128)S(1)}, u32[]{:S(2)}, u32[]{:S(2)}) async-start(f32[128,2,2056]{2,1,0:T(2,128)} %copy.108), calls=%async_computation.1 | async-start | bytes 4456448 | tf_op jit(solution)/shard_map/all_to_all | solution.py:36
  358.0 112.1 %all-to-all-start.2 = ((f32[128,2,2056]{2,1,0:T(2,128)}), f32[128,2,2056]{2,1,0:T(2,128)}, u32[]{:S(2)}, u32[]{:S(2)}) async-start(f32[128,2,2056]{2,1,0:T(2,128)} %copy.111), calls=%async_computation.2 | async-start | bytes 4456448 | tf_op jit(solution)/shard_map/all_to_all | solution.py:37
  520.2 67.7 %all-to-all-start.9 = ((f32[2,128,1028]{2,0,1:T(2,128)}), f32[2,128,1028]{2,0,1:T(2,128)}, u32[]{:S(2)}, u32[]{:S(2)}) async-start(f32[2,128,1028]{2,0,1:T(2,128)} %copy.146), calls=%async_computation.9 | async-start | bytes 2359296 | tf_op jit(solution)/shard_map/all_to_all | solution.py:65
  528.8 64.6 %copy-start.4 = (f32[1024,2,128]{2,0,1:T(8,128)S(1)}, f32[1024,2,128]{2,0,1:T(8,128)}, u32[]{:S(2)}) copy-start(f32[1024,2,128]{2,0,1:T(8,128)} %get-tuple-element.28) | copy-start | bytes 3145732
  587.9 67.1 %all-to-all-start.10 = ((f32[2,128,1028]{2,0,1:T(2,128)}), f32[2,128,1028]{2,0,1:T(2,128)}, u32[]{:S(2)}, u32[]{:S(2)}) async-start(f32[2,128,1028]{2,0,1:T(2,128)} %copy.149), calls=%async_computation.10 | async-start | bytes 2359296 | tf_op jit(solution)/shard_map/all_to_all | solution.py:66
  655.1 106.9 %all-to-all-start.3 = ((f32[2,128,2048]{2,0,1:T(2,128)}), f32[2,128,2048]{2,0,1:T(2,128)}, u32[]{:S(2)}, u32[]{:S(2)}) async-start(f32[2,128,2048]{2,0,1:T(2,128)} %copy.120), calls=%async_computation.3 | async-start | bytes 4194304 | tf_op jit(solution)/shard_map/all_to_all | solution.py:65
  761.9 106.3 %all-to-all-start.4 = ((f32[2,128,2048]{2,0,1:T(2,128)}), f32[2,128,2048]{2,0,1:T(2,128)S(1)}, u32[]{:S(2)}, u32[]{:S(2)}) async-start(f32[2,128,2048]{2,0,1:T(2,128)} %copy.126), calls=%async_computation.4 | async-start | bytes 4194304 | tf_op jit(solution)/shard_map/all_to_all | solution.py:66
  868.3 41.7 %all-to-all-start.11 = ((f32[64,2,1028]{2,1,0:T(2,128)}), f32[64,2,1028]{2,1,0:T(2,128)S(1)}, u32[]{:S(2)}, u32[]{:S(2)}) async-start(f32[64,2,1028]{2,1,0:T(2,128)} %copy.154), calls=%async_computation.11 | async-start | bytes 1179648 | tf_op jit(solution)/shard_map/all_to_all | solution.py:79
  891.4 23.9 %copy-start.21 = (bf16[1024,128]{1,0:T(8,128)(2,1)S(1)}, bf16[1024,128]{1,0:T(8,128)(2,1)}, u32[]{:S(2)}) copy-start(bf16[1024,128]{1,0:T(8,128)(2,1)} %param.16) | copy-start | bytes 786436
  910.0 60.5 %all-to-all-start.5 = ((f32[64,2,2048]{2,1,0:T(2,128)}), f32[64,2,2048]{2,1,0:T(2,128)S(1)}, u32[]{:S(2)}, u32[]{:S(2)}) async-start(f32[64,2,2048]{2,1,0:T(2,128)} %copy.128), calls=%async_computation.5 | async-start | bytes 2097152 | tf_op jit(solution)/shard_map/all_to_all | solution.py:79
  915.3 55.9 %copy-start.22 = (f32[1024]{0:T(1024)S(1)}, f32[1024]{0:T(1024)}, u32[]{:S(2)}) copy-start(f32[1024]{0:T(1024)} %param.15) | copy-start | bytes 12292
  915.3 55.9 %copy-start.23 = (f32[1024]{0:T(1024)S(1)}, f32[1024]{0:T(1024)}, u32[]{:S(2)}) copy-start(f32[1024]{0:T(1024)} %param.20) | copy-start | bytes 12292
  916.6 54.7 %copy-start.16 = (bf16[1024,128]{0,1:T(8,128)(2,1)S(1)}, bf16[1024,128]{0,1:T(8,128)(2,1)}, u32[]{:S(2)}) copy-start(bf16[1024,128]{0,1:T(8,128)(2,1)} %copy.129) | copy-start | bytes 786436
  (14 other events, 33.9 us)
where the time goes:
time: 993 us; the launch traced here: 977 us
  waiting for transfers between devices  727 us (73%)
  starting transfers between devices  82.4 us (8%)
  local copies, waits for them, and re-layouts  80.1 us (8%)
  matrix products  60.1 us (6%)
  blocking collectives  15.8 us (2%)
  other arithmetic  10.5 us (1%)
    all_to_all x2, waiting for transfers between devices, inverse_field(): lax.all_to_all(back_real, 'ctx', split_axis=1, concat_axis=0, tiled=True)  149 us
    all_to_all x2, waiting for transfers between devices, inverse_field(): lax.all_to_all(back_imag, 'ctx', split_axis=1, concat_axis=0, tiled=True)  145 us
    all_to_all x2, waiting for transfers between devices, forward_spectrum(): lax.all_to_all(turned_real, 'ctx', split_axis=0, concat_axis=1, tiled=True)  142 us
    all_to_all x2, waiting for transfers between devices, forward_spectrum(): lax.all_to_all(turned_imag, 'ctx', split_axis=0, concat_axis=1, tiled=True)  138 us
    all_to_all x2, waiting for transfers between devices, forward_spectrum(): lax.all_to_all(columns, 'ctx', split_axis=1, concat_axis=0, tiled=True)  82.1 us
    all_to_all x2, waiting for transfers between devices, inverse_field(): lax.all_to_all(local_values, 'ctx', split_axis=0, concat_axis=1, tiled=True)  70.1 us
    all_to_all x2, starting transfers between devices, forward_spectrum(): lax.all_to_all(columns, 'ctx', split_axis=1, concat_axis=0, tiled=True)  24 us
  transfers between devices with their start and end apart: 12, of which 12 were waited for; matrix products, arithmetic and copies ran while one was open for 10% of the time, Pallas kernels for 0%

commit v1 on v0

v1 whole, which is shorter than its diff:
```python
import jax
import jax.numpy as jnp
from jax import lax
from jax.sharding import PartitionSpec as P


def local(
    query_pol,
    keys_pol,
    value_pol,
    filter_pol,
    skip_pol,
    query_ref,
    keys_ref,
    value_ref,
    filter_ref,
    skip_ref,
    grad_out,
):
    chan_rows, span = query_pol.shape
    group_count = filter_pol.shape[0]
    gated_pol = keys_pol.astype(jnp.float32) * value_pol.astype(jnp.float32)
    gated_ref = keys_ref.astype(jnp.float32) * value_ref.astype(jnp.float32)
    out_grad = grad_out.astype(jnp.float32)
    grad_sum = out_grad * query_pol.astype(jnp.float32)

    stacked = jnp.stack([gated_pol, gated_ref, grad_sum])
    by_channel = lax.all_to_all(stacked, "ctx", split_axis=1, concat_axis=2, tiled=True)
    length = by_channel.shape[2]
    own_rows = by_channel.shape[1]
    filters = lax.all_gather(
        jnp.stack([filter_pol, filter_ref]), "ctx", axis=2, tiled=True
    )

    spec = jnp.fft.rfft(by_channel, n=2 * length, axis=-1)
    filt_spec = jnp.fft.rfft(filters, n=2 * length, axis=-1)
    grouped = spec.reshape(3, own_rows // group_count, group_count, -1)
    hpol = filt_spec[0][None]
    href = filt_spec[1][None]
    conv_pol = grouped[0] * hpol
    conv_ref = grouped[1] * href
    corr = grouped[2] * jnp.conj(hpol)
    cross = jnp.sum(grouped[2] * jnp.conj(grouped[0]), axis=0)
    prods = jnp.concatenate(
        [
            jnp.stack([conv_pol, conv_ref, corr]).reshape(3 * own_rows, -1),
            cross,
        ],
        axis=0,
    )
    fields = jnp.fft.irfft(prods, n=2 * length, axis=-1)[:, :length]
    back = fields[: 3 * own_rows].reshape(3, own_rows, length)
    partial_filter = fields[3 * own_rows :]

    returned = lax.all_to_all(back, "ctx", split_axis=2, concat_axis=1, tiled=True)
    grad_filter = lax.psum_scatter(partial_filter, "ctx", scatter_dimension=1, tiled=True)
    grad_filter = lax.psum(grad_filter, "chan")

    mix_pol = returned[0] + skip_pol[:, None] * gated_pol
    mix_ref = returned[1] + skip_ref[:, None] * gated_ref
    grad_mix = returned[2] + skip_pol[:, None] * grad_sum
    out_pol = (query_pol.astype(jnp.float32) * mix_pol).astype(jnp.bfloat16)
    out_ref = (query_ref.astype(jnp.float32) * mix_ref).astype(jnp.bfloat16)
    grad_query = (out_grad * mix_pol).astype(jnp.bfloat16)
    grad_keys = (grad_mix * value_pol.astype(jnp.float32)).astype(jnp.bfloat16)
    grad_value = (grad_mix * keys_pol.astype(jnp.float32)).astype(jnp.bfloat16)
    return (out_pol, out_ref, grad_query, grad_keys, grad_value, grad_filter)


def solution(mesh):
    in_specs = (
        P("chan", "ctx"),
        P("chan", "ctx"),
        P("chan", "ctx"),
        P(None, "ctx"),
        P("chan"),
        P("chan", "ctx"),
        P("chan", "ctx"),
        P("chan", "ctx"),
        P(None, "ctx"),
        P("chan"),
        P("chan", "ctx"),
    )
    out_specs = (
        P("chan", "ctx"),
        P("chan", "ctx"),
        P("chan", "ctx"),
        P("chan", "ctx"),
        P("chan", "ctx"),
        P(None, "ctx"),
    )
    return jax.shard_map(local, mesh=mesh, in_specs=in_specs, out_specs=out_specs, check_vma=False)
```

time: 993 us -> 751 us (0.76)
  waiting for transfers between devices: 727 us -> 226 us
  blocking collectives: 15.8 us -> 172 us
  local copies, waits for them, and re-layouts: 80.1 us -> 180 us
  starting transfers between devices: 82.4 us -> 34.1 us
  matrix products: 60.1 us -> 82.6 us
  other arithmetic: 10.5 us -> 26.8 us
  between operations: 1.65 us -> 14.8 us
    all_to_all x12 -> x2, waiting for transfers between devices: 727 us -> 0.01 us  [the longest x1 0.01 us: local(): lax.all_to_all(stacked, 'ctx', split_axis=1, concat_axis=2, tiled=True)]
    unnamed x0 -> x2, waiting for transfers between devices: none -> 226 us
    all_gather x0 -> x1, blocking collectives: none -> 156 us  [local(): lax.all_gather(jnp.stack([filter_pol, filter_ref]), 'ctx', axis=2, tiled=...]
    unnamed x67 -> x53, local copies, waits for them, and re-layouts: 11.5 us -> 117 us
    another operation x0 -> x18, matrix products: none -> 82.6 us  [the longest x6 37.8 us: local(): fields = jnp.fft.irfft(prods, n=2 * length, axis=-1)[:, :length]]
    dot_general x24 -> x0, matrix products: 60.1 us -> none  [the longest x2 7.39 us: forward_spectrum(): jnp.einsum('pnr,nf->pfr', moved_imag, sin_local, precision=HIGHEST)]
    all_to_all x12 -> x2, starting transfers between devices: 82.4 us -> 34.1 us  [the longest x1 18.9 us: local(): lax.all_to_all(stacked, 'ctx', split_axis=1, concat_axis=2, tiled=True)]
    another operation x0 -> x16, local copies, waits for them, and re-layouts: none -> 25.1 us  [the longest x6 9.71 us: local(): spec = jnp.fft.rfft(by_channel, n=2 * length, axis=-1)]
  transfers between devices with their start and end apart: 12 -> 3, of which waited for: 12 -> 1; matrix products, arithmetic and copies ran while one was open for 10% -> 3% of each run, Pallas kernels for 0% -> 0%
where the time goes in v1:
time: 751 us; the launch traced here: 736 us
  waiting for transfers between devices  226 us (30%)
  local copies, waits for them, and re-layouts  180 us (24%)
  blocking collectives  172 us (23%)
  matrix products  82.6 us (11%)
  starting transfers between devices  34.1 us (5%)
  other arithmetic  26.8 us (4%)
  between operations  14.8 us (2%)
    unnamed x2, waiting for transfers between devices  226 us
    all_gather x1, blocking collectives, local(): lax.all_gather(jnp.stack([filter_pol, filter_ref]), 'ctx', axis=2, tiled=...  156 us
    unnamed x53, local copies, waits for them, and re-layouts  117 us
    another operation x6, matrix products, local(): fields = jnp.fft.irfft(prods, n=2 * length, axis=-1)[:, :length]  37.8 us
    another operation x6, matrix products, local(): spec = jnp.fft.rfft(by_channel, n=2 * length, axis=-1)  34.3 us
    all_to_all x1, starting transfers between devices, local(): lax.all_to_all(stacked, 'ctx', split_axis=1, concat_axis=2, tiled=True)  18.9 us
    psum x1, blocking collectives, local(): grad_filter = lax.psum(grad_filter, 'chan')  16.1 us
    all_to_all x1, starting transfers between devices, local(): lax.all_to_all(back, 'ctx', split_axis=2, concat_axis=1, tiled=True)  15.2 us
  transfers between devices with their start and end apart: 3, of which 1 were waited for; matrix products, arithmetic and copies ran while one was open for 3% of the time, Pallas kernels for 0%

profile of v1, /device:TPU:6, one launch (start us, length us, event | category | flops | bytes accessed | tf_op | source)
XLA Modules:
  0.0 736.2 jit_solution(1127289093588753148)
XLA Ops:
  13.1 18.9 %all-to-all-start = ((f32[3,1024,128]{2,0,1:T(4,128)}), f32[3,1024,128]{2,0,1:T(4,128)S(1)}, u32[]{:S(2)}, u32[]{:S(2)}) async-start(f32[3,1024,128]{2,0,1:T(4,128)} %pad_maximum_fusion.2), calls=%async_computation | async-start | bytes 4194304 | tf_op jit(solution)/shard_map/all_to_all | solution.py:28
  34.0 156.2 %all_gather.3 = f32[2,4,8192]{2,1,0:T(4,128)S(1)} all-gather(f32[2,4,128]{2,1,0:T(4,128)S(1)} %pad_maximum_fusion.5), channel_id=1, replica_groups=mesh['ctx'=64,'chan'=8] {'ctx'}, dimensions={2}, use_global_device_ids=true | all-gather | bytes 266240 | tf_op jit(solution)/shard_map/all_gather | solution.py:31
  214.6 5.3 fusion.14
  223.0 5.8 fusion.26
  228.8 5.8 fusion.18
  234.7 7.3 add_bitcast_fusion
  242.0 7.0 subtract_bitcast_fusion
  285.6 31.5 %reverse.3 = f32[52,8192]{1,0:T(8,128)} reverse(f32[52,8192]{1,0:T(8,128)} %bitcast.238), dimensions={1} | reverse | bytes 3407872
  324.1 32.0 %reverse.2 = f32[52,8192]{1,0:T(8,128)} reverse(f32[52,8192]{1,0:T(8,128)} %bitcast.239), dimensions={1} | reverse | bytes 3407872
  360.9 5.8 fusion.4
  366.7 5.8 fusion.20
  372.5 5.6 fusion.23
  378.2 6.5 fusion.2
  384.6 5.9 fusion.36
  390.6 8.1 %multiply_bitcast_fusion = f32[52,128,128]{1,2,0:T(8,128)} fusion(f32[52,128,128]{2,1,0:T(8,128)S(1)} %fusion.2, f32[52,128,128]{2,1,0:T(8,128)S(1)} %fusion.36, f32[52,128,128]{2,1,0:T(8,128)S(1)} %fusion.20, f32[52,128,128]{2,1,0:T(8,128)S(1)} %fusion.23, f32[128,128]{0,1:T(8,128)S(1)} %copy-done.5, f32[128,128]{0,1:T(8,128)S(1)} %copy.84), kind=kOutput, calls=%fused_computation.8 | convolution fusion | flops 1315520512 | bytes 17170432 | tf_op jit(solution)/shard_map/jit(fft) | solution.py:51
  398.7 3.6 copy.90
  406.7 10.6 %copy.91 = f32[3,16,8192]{1,0,2:T(4,128)} copy(f32[3,16,8192]{2,1,0:T(8,128)S(1)} %bitcast.242) | data formatting | bytes 3145728 | tf_op jit(solution)/shard_map/reshape | solution.py:52
  417.3 17.0 %reshape.205 = f32[64,1,6144]{2,1,0:T(1,128)} reshape(f32[8192,3,16]{2,1,0:T(4,128)} %bitcast.222) | data formatting | bytes 3145728
  434.3 15.2 %all-to-all-start.1 = ((f32[64,1,6144]{2,1,0:T(1,128)}), f32[64,1,6144]{2,1,0:T(1,128)S(1)}, u32[]{:S(2)}, u32[]{:S(2)}) async-start(f32[64,1,6144]{2,1,0:T(1,128)} %reshape.205), calls=%async_computation.1 | async-start | bytes 3145728 | tf_op jit(solution)/shard_map/all_to_all | solution.py:55
  453.2 226.0 %reduce-scatter.5.cloned.1.call-done = f32[128,4]{1,0:T(8,128)} async-done(((f32[8192,4]{1,0:T(8,128)}), f32[128,4]{1,0:T(8,128)}) %reduce-scatter.5.cloned.1.call-update) | async-done | bytes 2064
  680.1 16.1 %psum.6 = f32[4,128]{1,0:T(4,128)} all-reduce(f32[4,128]{1,0:T(4,128)S(1)} %copy.113), channel_id=1, replica_groups=mesh['ctx'=64,'chan'=8] {'chan'}, use_global_device_ids=true, to_apply=%region_2.3 | all-reduce | flops 512 | bytes 4096 | tf_op jit(solution)/shard_map/psum | solution.py:57
  696.7 4.4 reduce.1
  701.1 12.7 %reshape.206 = f32[8192,3,16]{2,1,0:T(4,128)} reshape(f32[64,6144]{1,0:T(8,128)S(1)} %reduce.1) | data formatting | bytes 3145728
  713.8 11.8 %copy.92 = f32[3,16,64,128]{3,1,2,0:T(8,128)S(1)} copy(f32[3,16,64,128]{1,0,3,2:T(4,128)} %bitcast.223) | data formatting | bytes 3145728 | tf_op jit(solution)/shard_map/all_to_all | solution.py:55
  (116 shorter events, 96.3 us)
Async XLA Ops:
  13.1 20.9 %copy-start.15 = (f32[4,128]{1,0:T(4,128)S(1)}, f32[4,128]{1,0:T(4,128)}, u32[]{:S(2)}) copy-start(f32[4,128]{1,0:T(4,128)} %param.19) | copy-start | bytes 6148
  13.1 20.9 %copy-start.16 = (f32[4,128]{1,0:T(4,128)S(1)}, f32[4,128]{1,0:T(4,128)}, u32[]{:S(2)}) copy-start(f32[4,128]{1,0:T(4,128)} %param.14) | copy-start | bytes 6148
  13.1 196.9 %all-to-all-start = ((f32[3,1024,128]{2,0,1:T(4,128)}), f32[3,1024,128]{2,0,1:T(4,128)S(1)}, u32[]{:S(2)}, u32[]{:S(2)}) async-start(f32[3,1024,128]{2,0,1:T(4,128)} %pad_maximum_fusion.2), calls=%async_computation | async-start | bytes 4194304 | tf_op jit(solution)/shard_map/all_to_all | solution.py:28
  190.7 1.1 copy-start.4
  196.1 0.8 copy-start.3
  317.1 2.2 copy-start.1
  358.8 2.0 copy-start
  372.5 5.6 copy-start.5
  404.8 1.8 copy-start.2
  434.3 261.9 %all-to-all-start.1 = ((f32[64,1,6144]{2,1,0:T(1,128)}), f32[64,1,6144]{2,1,0:T(1,128)S(1)}, u32[]{:S(2)}, u32[]{:S(2)}) async-start(f32[64,1,6144]{2,1,0:T(1,128)} %reshape.205), calls=%async_computation.1 | async-start | bytes 3145728 | tf_op jit(solution)/shard_map/all_to_all | solution.py:55
  449.5 229.7 %reduce-scatter.5.cloned.1.call-start = ((), (), s32[]{:S(2)}) async-start(), calls=%async_computation.3 | async-start | bytes 4259840
  725.6 1.0 copy-start.6
  725.6 1.0 copy-start.7
  725.7 1.1 copy-start.8
  725.7 1.2 copy-start.9
  725.7 1.2 copy-start.13
  725.7 2.5 copy-start.10
  725.7 2.5 copy-start.11
  725.7 2.5 copy-start.12
  725.7 2.5 copy-start.14
Sparse Core Ops, SparseCore 0:
  455.0 224.1 reduce-scatter.4
